TPU v7x, 256 devices: a whole 4x4x8 slice. The times are simulated.
256 devices in a mesh: shard: 64 (over y, z, core), cent: 4 (over x).
Axes of the slice: x: 4, y: 4, z: 8, core: 2. Of those that a mesh axis runs over, the one named last changes fastest.
Arguments:
- queries: bfloat16 [1024, 32, 128], P('shard'), may hold values from -6 to 6
- centroids: bfloat16 [196608, 128], P(('shard', 'cent')), may hold values from -0.5 to 0.5
- passages: bfloat16 [16384, 128, 128], P('shard', 'cent'), may hold values from -0.5 to 0.5
- lengths: int32 [16384], P('shard'), may hold values from 16 to 128, as said below
- passage_row: int32 [16384], replicated, may hold values from 0 to 16383, as said below
- candidates: int32 [1024, 16], P('shard'), may hold values from 0 to 16383, as said below
Outputs:
- token_best: float32 [1024, 32], P('shard')
- scores: float32 [1024, 16], P('shard')
Inputs may be any that keep to these rules, and one draw needn't show every extreme that they name: A permutation: passage g is stored at row passage_row[g]. The rows j < lengths[r] of stored passage r are real, the rest padding; the first stored passage of every index of shard has all 128. Among the 256 pairs of the queries of one index of shard, at most 12 have candidates stored at one owner (owner = passage_row[id] // 256); one owner takes exactly 12 pairs from every index of shard.
All inputs are finite; a program needn't handle non-finite values.
Results may differ from a plain program's by a relative error of at most 0.0003.
Values may be sent and summed in bfloat16 or wider, within the bound.
No kernel may reach another device: no remote copies, remote signals or barrier semaphores. Data moves between devices by JAX's collectives and lax.ppermute only.
A program may use at most 128 MiB of HBM per device.

v0:
```python
import jax
import jax.numpy as jnp
from jax import lax
from jax.sharding import PartitionSpec as P

masked_score = -1e30


def per_device(queries, centroids, passages, lengths, passage_row, candidates):
    query_count = queries.shape[0]
    query_tokens = queries.shape[1]
    feature_width = queries.shape[2]
    per_query = candidates.shape[1]
    passage_count = passages.shape[0]
    token_rows = passages.shape[1]
    shard_total = lax.axis_size("shard")
    capacity = max(2, 3 * query_count * per_query // shard_total)
    my_shard = lax.axis_index("shard")
    query_block = lax.all_gather(queries, "shard", axis=0, tiled=True)
    flattened = query_block.reshape(-1, feature_width)
    scored = jnp.einsum("rd,cd->rc", flattened, centroids, preferred_element_type=jnp.float32)
    local_best = jnp.max(scored, axis=1).reshape(query_block.shape[0], query_tokens)
    merged = lax.pmax(local_best, ("shard", "cent"))
    token_best = lax.dynamic_slice_in_dim(merged, my_shard * query_count, query_count, 0)
    pair_rows = jnp.take(passage_row, candidates.reshape(-1), axis=0)
    owners = pair_rows // passage_count
    slot_ids = pair_rows % passage_count
    onehot = (owners[:, None] == jnp.arange(shard_total, dtype=jnp.int32)[None, :]).astype(
        jnp.int32
    )
    ranking = jnp.sum((jnp.cumsum(onehot, axis=0) - onehot) * onehot, axis=1)
    places = owners * capacity + ranking
    pair_query = jnp.arange(query_count * per_query, dtype=jnp.int32) // per_query
    slot_table = (
        jnp.full((shard_total * capacity,), -1, jnp.int32)
        .at[places]
        .set(slot_ids)
        .reshape(shard_total, capacity)
    )
    token_index = lax.axis_index("cent") * token_rows + jnp.arange(token_rows, dtype=jnp.int32)
    flat_queries = queries.reshape(query_count, query_tokens * feature_width)
    token_table = jnp.zeros((shard_total * capacity, query_tokens * feature_width), jnp.bfloat16)
    token_table = token_table.at[places].set(jnp.take(flat_queries, pair_query, axis=0))
    token_table = token_table.reshape(shard_total, capacity, query_tokens * feature_width)
    slot_block = lax.all_to_all(slot_table, "shard", split_axis=0, concat_axis=0, tiled=True)
    safe_slots = jnp.maximum(slot_block, 0).reshape(-1)
    chosen = jnp.take(passages, safe_slots, axis=0)
    asked = lax.all_to_all(token_table, "shard", split_axis=0, concat_axis=0, tiled=True).reshape(
        -1, query_tokens, feature_width
    )
    scored = jnp.einsum("ntd,npd->ntp", asked, chosen, preferred_element_type=jnp.float32)
    valid_tokens = token_index[None, :] < jnp.take(lengths, safe_slots, axis=0)[:, None]
    scored = jnp.where(valid_tokens[:, None, :], scored, masked_score)
    partial_value = jnp.max(scored, axis=2).reshape(
        slot_block.shape[0], slot_block.shape[1], query_tokens
    )
    complete = lax.pmax(partial_value, "cent")
    pair_scores = jnp.sum(complete, axis=2) / query_tokens
    returned = lax.all_to_all(pair_scores, "shard", split_axis=0, concat_axis=0, tiled=True)
    scores = jnp.take(returned.reshape(-1), places, axis=0).reshape(query_count, per_query)
    return (token_best, scores)


def solution(mesh):
    in_specs = (
        P("shard", None, None),
        P(("shard", "cent"), None),
        P("shard", "cent", None),
        P("shard"),
        P(),
        P("shard", None),
    )
    out_specs = (P("shard", None), P("shard", None))
    return jax.shard_map(
        per_device, mesh=mesh, in_specs=in_specs, out_specs=out_specs, check_vma=False
    )
```

profile of v0, /device:TPU:2, one launch (start us, length us, event | category | flops | bytes accessed | tf_op | source)
XLA Modules:
  0.0 633.1 jit_solution(10304121452053333185)
XLA Ops:
  8.0 0.0 copy-start
  8.0 0.9 reshape.321
  8.9 0.8 reshape.322
  9.7 0.8 reshape.323
  10.5 2.1 gather_fusion
  12.7 0.6 reduce-window.6
  13.3 0.2 slice_reduce_fusion
  13.5 0.1 fusion.13
  13.6 1.4 scatter_custom_fusion
  15.0 0.7 all_to_all.13
  15.7 12.3 %all-to-all-start = ((s32[64,1,12]{2,1,0:T(1,128)}), s32[64,1,12]{2,1,0:T(1,128)S(1)}, u32[]{:S(2)}, u32[]{:S(2)}) async-start(s32[64,1,12]{2,1,0:T(1,128)} %bitcast.7), calls=%async_computation | async-start | bytes 65536 | tf_op jit(solution)/shard_map/all_to_all | solution.py:45
  28.1 1.0 copy.15
  29.0 13.4 %scatter_custom_fusion.1 = bf16[768,4096]{1,0:T(8,128)(2,1)} fusion(s32[256]{0:T(256)S(1)} %bitcast.44, bf16[]{:T(256)} %constant.143.clone.1, pred[256]{0:T(512)(128)(4,1)S(1)} %compare_and_fusion, bf16[]{:T(256)} %constant.146.clone.1, bf16[16,4096]{1,0:T(8,128)(2,1)S(1)} %bitcast.38, s32[1024]{0:T(1024)S(1)} %pad_clamp_fusion.1), kind=kCustom, calls=%fused_computation.13 | custom fusion | flops 1048576 | bytes 6427140 | tf_op jit(solution)/shard_map/scatter | solution.py:43
  42.5 9.8 %reshape.326 = bf16[64,12,4096]{2,1,0:T(8,128)(2,1)} reshape(bf16[768,4096]{1,0:T(8,128)(2,1)} %scatter_custom_fusion.1) | data formatting | bytes 12582912 | tf_op jit(solution)/shard_map/reshape | solution.py:44
  52.2 0.0 copy-start.1
  52.2 0.0 all-to-all-done
  52.2 10.5 %all-to-all-start.1 = ((bf16[64,12,4096]{2,1,0:T(8,128)(2,1)}), bf16[64,12,4096]{2,1,0:T(8,128)(2,1)}, u32[]{:S(2)}, u32[]{:S(2)}) async-start(bf16[64,12,4096]{2,1,0:T(8,128)(2,1)} %reshape.326), calls=%async_computation.1 | async-start | bytes 16777216 | tf_op jit(solution)/shard_map/all_to_all | solution.py:48
  62.8 0.0 all-reduce.5.cloned.1.call-start
  62.9 0.1 compare_reduce_fusion
  63.0 0.1 le.92
  63.1 0.1 maximum_reduce_fusion
  63.2 0.1 reshape.340
  63.3 0.0 copy-done.1
  63.3 5.0 gather_fusion.1
  68.3 0.0 copy-done
  68.3 4.4 gather_fusion.2
  72.8 0.2 broadcast_compare_fusion
  73.0 174.6 %all-to-all-done.1 = bf16[64,12,4096]{2,1,0:T(8,128)(2,1)} async-done(((bf16[64,12,4096]{2,1,0:T(8,128)(2,1)}), bf16[64,12,4096]{2,1,0:T(8,128)(2,1)}, u32[]{:S(2)}, u32[]{:S(2)}) %all-to-all-start.1) | async-done | bytes 6291488 | tf_op jit(solution)/shard_map/all_to_all | solution.py:48
  247.6 12.2 %reshape.327 = bf16[768,32,128]{2,1,0:T(8,128)(2,1)} reshape(bf16[64,12,4096]{2,1,0:T(8,128)(2,1)} %all-to-all-done.1) | data formatting | bytes 12582912 | tf_op jit(solution)/shard_map/reshape | solution.py:48
  259.7 0.0 copy-start.3
  259.8 9.2 %select_reduce_fusion = f32[768,32]{1,0:T(8,128)S(1)} fusion(pred[768,32]{1,0:T(8,128)(4,1)S(1)} %broadcast_compare_fusion, bf16[768,32,128]{2,1,0:T(8,128)(2,1)} %reshape.327, bf16[768,32,128]{2,1,0:T(8,128)(2,1)} %gather_fusion.2, pred[768]{0:T(1024)(128)(4,1)S(1)} %le.92), kind=kOutput, calls=%fused_computation.8 | convolution fusion | flops 206020608 | bytes 12706560 | tf_op jit(solution)/shard_map/ntd,npd->ntp/dot_general | solution.py:51
  268.9 0.9 reshape.328
  269.8 0.0 all-reduce.5.cloned.1.call-update
  269.8 0.0 all-gather.2.cloned.1.call-start
  269.9 0.5 all-gather.2.cloned.1.call-update
  270.4 44.4 %all-reduce.5.cloned.1.call-done = f32[64,12,32]{2,1,0:T(8,128)} async-done(((f32[64,12,32]{2,1,0:T(8,128)}), f32[64,12,32]{2,1,0:T(8,128)}) %all-reduce.5.cloned.1.call-update) | async-done | bytes 98320 | tf_op jit(solution)/shard_map/pmax | solution.py:57
  314.8 1.3 reduce_sum.25
  316.0 0.6 broadcast_multiply_fusion
  316.6 10.5 %all-to-all-start.2 = ((f32[64,1,12]{2,1,0:T(1,128)}), f32[64,1,12]{2,1,0:T(1,128)S(1)}, u32[]{:S(2)}, u32[]{:S(2)}) async-start(f32[64,1,12]{2,1,0:T(1,128)} %bitcast.9), calls=%async_computation.2 | async-start | bytes 65536 | tf_op jit(solution)/shard_map/all_to_all | solution.py:59
  327.1 0.3 all-reduce.3.cloned.1.call-start
  327.5 0.1 reduce_sum.23
  327.5 0.1 gather.29
  327.6 9.1 %all-to-all-done.2 = f32[64,1,12]{2,1,0:T(1,128)S(1)} async-done(((f32[64,1,12]{2,1,0:T(1,128)}), f32[64,1,12]{2,1,0:T(1,128)S(1)}, u32[]{:S(2)}, u32[]{:S(2)}) %all-to-all-start.2) | async-done | bytes 3104 | tf_op jit(solution)/shard_map/all_to_all | solution.py:59
  336.7 0.5 broadcast.432
  337.2 0.7 reduce.11
  337.9 0.1 reshape.329
  338.0 1.4 gather_fusion.3
  339.4 0.1 gather.36
  339.5 14.4 %all-gather.2.cloned.1.call-done = bf16[1024,32,128]{2,1,0:T(8,128)(2,1)} async-done(((bf16[16,32,128]{2,1,0:T(8,128)(2,1)}), bf16[1024,32,128]{2,1,0:T(8,128)(2,1)}) %all-gather.2.cloned.1.call-update) | async-done | bytes 8388624 | tf_op jit(solution)/shard_map/all_gather | solution.py:19
  353.9 0.0 copy-done.3
  353.9 0.0 copy-start.2
  353.9 17.0 %convolution_reduce_fusion = f32[32768]{0:T(1024)S(1)} fusion(bf16[32768,128]{1,0:T(8,128)(2,1)} %bitcast.47, bf16[768,128]{1,0:T(8,128)(2,1)S(1)} %copy-done.3), kind=kOutput, calls=%fused_computation.7 | convolution fusion | flops 6467584000 | bytes 8716288 | tf_op jit(solution)/shard_map/rd,cd->rc/dot_general | solution.py:21
  370.9 1.0 reshape.320
  371.9 0.0 all-reduce.3.cloned.1.call-update
  371.9 0.0 copy-done.2
  371.9 0.6 and_select_fusion
  372.6 251.8 %all-reduce.3.cloned.1.call-done = f32[1024,32]{1,0:T(8,128)} async-done(((f32[1024,32]{1,0:T(8,128)}), f32[1024,32]{1,0:T(8,128)}) %all-reduce.3.cloned.1.call-update) | async-done | bytes 131088 | tf_op jit(solution)/shard_map/pmax | solution.py:23
  624.3 1.3 constant_dynamic-slice_fusion
  (16 shorter events, 0.2 us)
Async XLA Ops:
  8.0 60.3 %copy-start = (bf16[256,32,128]{2,1,0:T(8,128)(2,1)S(1)}, bf16[256,32,128]{2,1,0:T(8,128)(2,1)}, u32[]{:S(2)}) copy-start(bf16[256,32,128]{2,1,0:T(8,128)(2,1)} %param.8) | copy-start | bytes 6291460
  15.7 36.5 %all-to-all-start = ((s32[64,1,12]{2,1,0:T(1,128)}), s32[64,1,12]{2,1,0:T(1,128)S(1)}, u32[]{:S(2)}, u32[]{:S(2)}) async-start(s32[64,1,12]{2,1,0:T(1,128)} %bitcast.7), calls=%async_computation | async-start | bytes 65536 | tf_op jit(solution)/shard_map/all_to_all | solution.py:45
  52.2 11.1 %copy-start.1 = (s32[256]{0:T(256)S(1)}, s32[256]{0:T(256)}, u32[]{:S(2)}) copy-start(s32[256]{0:T(256)} %param.9) | copy-start | bytes 3076
  52.2 195.3 %all-to-all-start.1 = ((bf16[64,12,4096]{2,1,0:T(8,128)(2,1)}), bf16[64,12,4096]{2,1,0:T(8,128)(2,1)}, u32[]{:S(2)}, u32[]{:S(2)}) async-start(bf16[64,12,4096]{2,1,0:T(8,128)(2,1)} %reshape.326), calls=%async_computation.1 | async-start | bytes 16777216 | tf_op jit(solution)/shard_map/all_to_all | solution.py:48
  62.8 252.0 %all-reduce.5.cloned.1.call-start = ((), (), s32[]{:S(2)}) async-start(), calls=%async_computation.5 | async-start | bytes 1048576 | tf_op jit(solution)/shard_map/pmax | solution.py:57
  259.7 94.1 %copy-start.3 = (bf16[768,128]{1,0:T(8,128)(2,1)S(1)}, bf16[768,128]{1,0:T(8,128)(2,1)}, u32[]{:S(2)}) copy-start(bf16[768,128]{1,0:T(8,128)(2,1)} %param.7) | copy-start | bytes 589828
  269.8 84.0 %all-gather.2.cloned.1.call-start = ((), (), s32[]{:S(2)}) async-start(), calls=%async_computation.3 | async-start | bytes 8519680 | tf_op jit(solution)/shard_map/all_gather | solution.py:19
  316.6 20.0 %all-to-all-start.2 = ((f32[64,1,12]{2,1,0:T(1,128)}), f32[64,1,12]{2,1,0:T(1,128)S(1)}, u32[]{:S(2)}, u32[]{:S(2)}) async-start(f32[64,1,12]{2,1,0:T(1,128)} %bitcast.9), calls=%async_computation.2 | async-start | bytes 65536 | tf_op jit(solution)/shard_map/all_to_all | solution.py:59
  327.1 297.2 %all-reduce.3.cloned.1.call-start = ((), (), s32[]{:S(2)}) async-start(), calls=%async_computation.4 | async-start | bytes 1048576 | tf_op jit(solution)/shard_map/pmax | solution.py:23
  353.9 18.1 %copy-start.2 = (s32[16,16]{1,0:T(8,128)S(1)}, s32[16,16]{1,0:T(8,128)}, u32[]{:S(2)}) copy-start(s32[16,16]{1,0:T(8,128)} %param.11) | copy-start | bytes 3076
Sparse Core Ops, SparseCore 0:
  270.0 44.7 all-reduce.4
Sparse Core Ops, SparseCore 1:
  273.1 80.7 all-gather.1
  372.0 252.3 all-reduce.2
where the time goes:
time: 634 us; the launch traced here: 633 us
  waiting for transfers between devices  495 us (78%)
  local copies, waits for them, and re-layouts  44.8 us (7%)
  starting transfers between devices  33.7 us (5%)
  matrix products  26.2 us (4%)
  other arithmetic  17.9 us (3%)
  between operations  15.7 us (2%)
    pmax x1, waiting for transfers between devices, per_device(): merged = lax.pmax(local_best, ('shard', 'cent'))  252 us
    all_to_all x1, waiting for transfers between devices, per_device(): lax.all_to_all(token_table, 'shard', split_axis=0, concat_axis=0, tiled=T...  175 us
    pmax x1, waiting for transfers between devices, per_device(): complete = lax.pmax(partial_value, 'cent')  44.4 us
    dot_general x1, matrix products, per_device(): jnp.einsum('rd,cd->rc', flattened, centroids, preferred_element_type=jnp....  17 us
    all_gather x1, waiting for transfers between devices, per_device(): query_block = lax.all_gather(queries, 'shard', axis=0, tiled=True)  14.4 us
    scatter x1, other arithmetic, per_device(): token_table.at[places].set(jnp.take(flat_queries, pair_query, axis=0))  13.4 us
  transfers between devices with their start and end apart: 6, of which 5 were waited for; matrix products, arithmetic and copies ran while one was open for 6% of the time, Pallas kernels for 0%

commit v1 on v0

--- a/solution.py
+++ b/solution.py
@@ -16,7 +16,9 @@
     shard_total = lax.axis_size("shard")
     capacity = max(2, 3 * query_count * per_query // shard_total)
     my_shard = lax.axis_index("shard")
-    query_block = lax.all_gather(queries, "shard", axis=0, tiled=True)
+    query_block = jnp.concatenate(
+        lax.all_to_all(jnp.stack([queries] * lax.axis_size("shard")), "shard", 0, 0), axis=0
+    )
     flattened = query_block.reshape(-1, feature_width)
     scored = jnp.einsum("rd,cd->rc", flattened, centroids, preferred_element_type=jnp.float32)
     local_best = jnp.max(scored, axis=1).reshape(query_block.shape[0], query_tokens)

time: 634 us -> 813 us (1.28)
  waiting for transfers between devices: 495 us -> 654 us
  blocking collectives: 0 us -> 19.8 us
    all_to_all x1, waiting for transfers between devices: 9.06 us -> 181 us  [per_device(): lax.all_to_all(jnp.stack([queries] * lax.axis_size('shard')), 'shard', 0, 0)]
    all_to_all x0 -> x1, blocking collectives: none -> 19.8 us  [per_device(): lax.all_to_all(pair_scores, 'shard', split_axis=0, concat_axis=0, tiled=T...]
    all_gather x1 -> x0, waiting for transfers between devices: 14.4 us -> none  [per_device(): query_block = lax.all_gather(queries, 'shard', axis=0, tiled=True)]
  transfers between devices with their start and end apart: 6 -> 5, of which waited for: 5 -> 4; matrix products, arithmetic and copies ran while one was open for 6% -> 5% of each run, Pallas kernels for 0% -> 0%
where the time goes in v1:
time: 813 us; the launch traced here: 812 us
  waiting for transfers between devices  654 us (80%)
  local copies, waits for them, and re-layouts  50 us (6%)
  starting transfers between devices  29.1 us (4%)
  matrix products  26.2 us (3%)
  blocking collectives  19.8 us (2%)
  other arithmetic  17.3 us (2%)
  between operations  15.7 us (2%)
    pmax x1, waiting for transfers between devices, per_device(): merged = lax.pmax(local_best, ('shard', 'cent'))  253 us
    all_to_all x1, waiting for transfers between devices, per_device(): lax.all_to_all(jnp.stack([queries] * lax.axis_size('shard')), 'shard', 0, 0)  181 us
    all_to_all x1, waiting for transfers between devices, per_device(): lax.all_to_all(token_table, 'shard', split_axis=0, concat_axis=0, tiled=T...  175 us
    pmax x1, waiting for transfers between devices, per_device(): complete = lax.pmax(partial_value, 'cent')  44.9 us
    all_to_all x1, blocking collectives, per_device(): lax.all_to_all(pair_scores, 'shard', split_axis=0, concat_axis=0, tiled=T...  19.8 us
    dot_general x1, matrix products, per_device(): jnp.einsum('rd,cd->rc', flattened, centroids, preferred_element_type=jnp....  17 us
  transfers between devices with their start and end apart: 5, of which 4 were waited for; matrix products, arithmetic and copies ran while one was open for 5% of the time, Pallas kernels for 0%

profile of v1, /device:TPU:2, one launch (start us, length us, event | category | flops | bytes accessed | tf_op | source)
XLA Modules:
  0.0 811.6 jit_solution(5544679996412878956)
XLA Ops:
  8.0 0.0 copy-start
  8.0 0.9 reshape.319
  8.9 0.8 reshape.320
  9.7 0.8 reshape.321
  10.5 2.1 gather_fusion
  12.7 0.6 reduce-window.6
  13.3 0.2 slice_reduce_fusion
  13.5 0.1 fusion.13
  13.6 1.4 scatter_custom_fusion
  15.0 0.7 all_to_all.17
  15.7 12.3 %all-to-all-start.1 = ((s32[64,1,12]{2,1,0:T(1,128)}), s32[64,1,12]{2,1,0:T(1,128)S(1)}, u32[]{:S(2)}, u32[]{:S(2)}) async-start(s32[64,1,12]{2,1,0:T(1,128)} %bitcast.7), calls=%async_computation.1 | async-start | bytes 65536 | tf_op jit(solution)/shard_map/all_to_all | solution.py:47
  28.1 1.0 copy.15
  29.0 13.4 %scatter_custom_fusion.1 = bf16[768,4096]{1,0:T(8,128)(2,1)} fusion(s32[256]{0:T(256)S(1)} %bitcast.45, bf16[]{:T(256)} %constant.143.clone.1, pred[256]{0:T(512)(128)(4,1)S(1)} %compare_and_fusion, bf16[]{:T(256)} %constant.146.clone.1, bf16[16,4096]{1,0:T(8,128)(2,1)S(1)} %bitcast.39, s32[1024]{0:T(1024)S(1)} %pad_clamp_fusion.1), kind=kCustom, calls=%fused_computation.13 | custom fusion | flops 1048576 | bytes 6427140 | tf_op jit(solution)/shard_map/scatter | solution.py:45
  42.5 9.8 %reshape.324 = bf16[64,12,4096]{2,1,0:T(8,128)(2,1)} reshape(bf16[768,4096]{1,0:T(8,128)(2,1)} %scatter_custom_fusion.1) | data formatting | bytes 12582912 | tf_op jit(solution)/shard_map/reshape | solution.py:46
  52.2 0.0 copy-start.1
  52.2 0.0 all-to-all-done.1
  52.2 10.5 %all-to-all-start.2 = ((bf16[64,12,4096]{2,1,0:T(8,128)(2,1)}), bf16[64,12,4096]{2,1,0:T(8,128)(2,1)}, u32[]{:S(2)}, u32[]{:S(2)}) async-start(bf16[64,12,4096]{2,1,0:T(8,128)(2,1)} %reshape.324), calls=%async_computation.2 | async-start | bytes 16777216 | tf_op jit(solution)/shard_map/all_to_all | solution.py:50
  62.8 0.0 all-reduce.5.cloned.1.call-start
  62.9 0.1 compare_reduce_fusion
  63.0 0.1 le.92
  63.1 0.1 maximum_reduce_fusion
  63.2 0.1 reshape.338
  63.3 0.0 copy-done.1
  63.3 5.0 gather_fusion.1
  68.3 0.0 copy-done
  68.3 4.4 gather_fusion.2
  72.8 0.2 broadcast_compare_fusion
  73.0 174.6 %all-to-all-done.2 = bf16[64,12,4096]{2,1,0:T(8,128)(2,1)} async-done(((bf16[64,12,4096]{2,1,0:T(8,128)(2,1)}), bf16[64,12,4096]{2,1,0:T(8,128)(2,1)}, u32[]{:S(2)}, u32[]{:S(2)}) %all-to-all-start.2) | async-done | bytes 6291488 | tf_op jit(solution)/shard_map/all_to_all | solution.py:50
  247.6 12.2 %reshape.325 = bf16[768,32,128]{2,1,0:T(8,128)(2,1)} reshape(bf16[64,12,4096]{2,1,0:T(8,128)(2,1)} %all-to-all-done.2) | data formatting | bytes 12582912 | tf_op jit(solution)/shard_map/reshape | solution.py:50
  259.7 0.0 copy-start.2
  259.8 9.1 %select_reduce_fusion = f32[768,32]{1,0:T(8,128)S(1)} fusion(pred[768,32]{1,0:T(8,128)(4,1)S(1)} %broadcast_compare_fusion, bf16[768,32,128]{2,1,0:T(8,128)(2,1)} %reshape.325, bf16[768,32,128]{2,1,0:T(8,128)(2,1)} %gather_fusion.2, pred[768]{0:T(1024)(128)(4,1)S(1)} %le.92), kind=kOutput, calls=%fused_computation.8 | convolution fusion | flops 206020608 | bytes 12706560 | tf_op jit(solution)/shard_map/ntd,npd->ntp/dot_general | solution.py:53
  268.9 0.8 reshape.326
  269.7 0.0 all-reduce.5.cloned.1.call-update
  269.8 44.9 %all-reduce.5.cloned.1.call-done = f32[64,12,32]{2,1,0:T(8,128)} async-done(((f32[64,12,32]{2,1,0:T(8,128)}), f32[64,12,32]{2,1,0:T(8,128)}) %all-reduce.5.cloned.1.call-update) | async-done | bytes 98320 | tf_op jit(solution)/shard_map/pmax | solution.py:59
  314.7 1.3 reduce_sum.25
  315.9 19.8 %all_to_all.25 = f32[64,1,12]{2,1,0:T(1,128)S(1)} all-to-all(f32[64,1,12]{2,1,0:T(1,128)S(1)} %bitcast.40), channel_id=1, replica_groups=mesh['shard'=64,'cent'=4] {'shard'}, dimensions={0} | all-to-all | bytes 6144 | tf_op jit(solution)/shard_map/all_to_all | solution.py:61
  335.7 0.0 copy-done.2
  335.7 5.2 stack.2
  341.0 0.0 copy-start.4
  341.0 5.9 all-to-all-start
  346.9 0.3 all-reduce.3.cloned.1.call-start
  347.2 0.1 reduce_sum.23
  347.2 0.1 gather.29
  347.3 0.5 broadcast.434
  347.9 0.7 reduce.11
  348.6 0.1 reshape.327
  348.7 1.4 gather_fusion.3
  350.1 0.1 gather.36
  350.1 181.5 %all-to-all-done = bf16[64,16,32,128]{3,2,1,0:T(8,128)(2,1)} async-done(((bf16[64,16,32,128]{3,2,1,0:T(8,128)(2,1)}), bf16[64,16,32,128]{3,2,1,0:T(8,128)(2,1)}, u32[]{:S(2)}, u32[]{:S(2)}) %all-to-all-start) | async-done | bytes 8388640 | tf_op jit(solution)/shard_map/all_to_all | solution.py:20
  531.6 0.0 copy-done.4
  531.6 0.0 copy-start.3
  531.6 17.0 %convolution_reduce_fusion = f32[32768]{0:T(1024)S(1)} fusion(bf16[32768,128]{1,0:T(8,128)(2,1)} %bitcast, bf16[768,128]{1,0:T(8,128)(2,1)S(1)} %copy-done.4), kind=kOutput, calls=%fused_computation.7 | convolution fusion | flops 6467584000 | bytes 8716288 | tf_op jit(solution)/shard_map/rd,cd->rc/dot_general | solution.py:23
  548.7 1.0 reshape.318
  549.7 0.0 all-reduce.3.cloned.1.call-update
  549.7 0.0 copy-done.3
  549.7 0.6 and_select_fusion
  550.3 252.5 %all-reduce.3.cloned.1.call-done = f32[1024,32]{1,0:T(8,128)} async-done(((f32[1024,32]{1,0:T(8,128)}), f32[1024,32]{1,0:T(8,128)}) %all-reduce.3.cloned.1.call-update) | async-done | bytes 131088 | tf_op jit(solution)/shard_map/pmax | solution.py:25
  802.9 1.3 constant_dynamic-slice_fusion
  (17 shorter events, 0.2 us)
Async XLA Ops:
  8.0 60.3 %copy-start = (bf16[256,32,128]{2,1,0:T(8,128)(2,1)S(1)}, bf16[256,32,128]{2,1,0:T(8,128)(2,1)}, u32[]{:S(2)}) copy-start(bf16[256,32,128]{2,1,0:T(8,128)(2,1)} %param.8) | copy-start | bytes 6291460
  15.7 36.5 %all-to-all-start.1 = ((s32[64,1,12]{2,1,0:T(1,128)}), s32[64,1,12]{2,1,0:T(1,128)S(1)}, u32[]{:S(2)}, u32[]{:S(2)}) async-start(s32[64,1,12]{2,1,0:T(1,128)} %bitcast.7), calls=%async_computation.1 | async-start | bytes 65536 | tf_op jit(solution)/shard_map/all_to_all | solution.py:47
  52.2 11.1 %copy-start.1 = (s32[256]{0:T(256)S(1)}, s32[256]{0:T(256)}, u32[]{:S(2)}) copy-start(s32[256]{0:T(256)} %param.9) | copy-start | bytes 3076
  52.2 195.3 %all-to-all-start.2 = ((bf16[64,12,4096]{2,1,0:T(8,128)(2,1)}), bf16[64,12,4096]{2,1,0:T(8,128)(2,1)}, u32[]{:S(2)}, u32[]{:S(2)}) async-start(bf16[64,12,4096]{2,1,0:T(8,128)(2,1)} %reshape.324), calls=%async_computation.2 | async-start | bytes 16777216 | tf_op jit(solution)/shard_map/all_to_all | solution.py:50
  62.8 251.9 %all-reduce.5.cloned.1.call-start = ((), (), s32[]{:S(2)}) async-start(), calls=%async_computation.5 | async-start | bytes 1048576 | tf_op jit(solution)/shard_map/pmax | solution.py:59
  259.7 76.0 %copy-start.2 = (bf16[16,32,128]{2,1,0:T(8,128)(2,1)S(1)}, bf16[16,32,128]{2,1,0:T(8,128)(2,1)}, u32[]{:S(2)}) copy-start(bf16[16,32,128]{2,1,0:T(8,128)(2,1)} %param.6) | copy-start | bytes 393220
  341.0 190.7 %copy-start.4 = (bf16[768,128]{1,0:T(8,128)(2,1)S(1)}, bf16[768,128]{1,0:T(8,128)(2,1)}, u32[]{:S(2)}) copy-start(bf16[768,128]{1,0:T(8,128)(2,1)} %param.7) | copy-start | bytes 589828
  341.0 190.7 %all-to-all-start = ((bf16[64,16,32,128]{3,2,1,0:T(8,128)(2,1)}), bf16[64,16,32,128]{3,2,1,0:T(8,128)(2,1)}, u32[]{:S(2)}, u32[]{:S(2)}) async-start(bf16[64,16,32,128]{3,2,1,0:T(8,128)(2,1)} %stack.2), calls=%async_computation | async-start | bytes 16777216 | tf_op jit(solution)/shard_map/all_to_all | solution.py:20
  346.9 456.0 %all-reduce.3.cloned.1.call-start = ((), (), s32[]{:S(2)}) async-start(), calls=%async_computation.4 | async-start | bytes 1048576 | tf_op jit(solution)/shard_map/pmax | solution.py:25
  531.6 18.1 %copy-start.3 = (s32[16,16]{1,0:T(8,128)S(1)}, s32[16,16]{1,0:T(8,128)}, u32[]{:S(2)}) copy-start(s32[16,16]{1,0:T(8,128)} %param.11) | copy-start | bytes 3076
Sparse Core Ops, SparseCore 0:
  269.9 44.7 all-reduce.4
Sparse Core Ops, SparseCore 1:
  549.8 253.0 all-reduce.2
